TPU v7x, 512 devices: a whole 4x8x8 slice. The times are simulated.
512 devices in a mesh: section: 32 (over z, x), neuron: 16 (over y, core).
Axes of the slice: x: 4, y: 8, z: 8, core: 2. Of those that a mesh axis runs over, the one named last changes fastest.
Arguments:
- inputs: bfloat16 [6, 32768], P(None, 'neuron'), may hold values from 0 to 2
- weight_tiles: bfloat16 [32, 2048, 128, 128], P('section', 'neuron'), may hold values from -0.07324219 to 0.07910156
- source_block: int32 [32, 2048], P('section', 'neuron'), may hold values from 0 to 255
- target_block: int32 [32, 2048], P('section', 'neuron'), may hold values from 0 to 15
- live_slots: int32 [32, 16], P('section', 'neuron'), may hold values from 16 to 128, as said below
Outputs:
- activations: bfloat16 [32, 6, 32768], P('section', None, 'neuron')
Inputs may be any that keep to these rules, and one draw needn't show every extreme that they name: live_slots[l, n] is 128, 64, 32 or 16, and in every layer some shard has all 128 slots live.
All inputs are finite; a program needn't handle non-finite values.
Results may differ from a plain program's by a relative error of at most 0.0045.
Values may be sent and summed in bfloat16 or wider, within the bound.
No kernel may reach another device: no remote copies, remote signals or barrier semaphores. Data moves between devices by JAX's collectives and lax.ppermute only.
A program may use at most 64 MiB of HBM per device.

v0:
```python
import jax
import jax.numpy as jnp
from jax import lax
from jax.sharding import PartitionSpec as P

NEURON_BIAS = -0.3
CLIP_LEVEL = 32.0
UNROLL = True


def layer_apply(gathered, weight_tiles, source, selector):
    row_count = gathered.shape[0]
    block_size = weight_tiles.shape[2]
    column_count = selector.shape[1]
    block_count = gathered.shape[1] // block_size
    shaped = gathered.reshape(row_count, block_count, block_size)
    picked = shaped.at[:, source].get(mode="promise_in_bounds")
    partial_value = jnp.einsum(
        "msk,skj->msj", picked, weight_tiles[0], preferred_element_type=jnp.float32
    )
    summed = jnp.einsum("msj,sc->mcj", partial_value, selector, precision=lax.Precision.HIGHEST)
    result = jnp.clip(summed + NEURON_BIAS, 0.0, CLIP_LEVEL).astype(jnp.bfloat16)
    return result.reshape(row_count, column_count * block_size)


def local(inputs, weight_tiles, source_block, target_block, live_slots):
    section_pos = lax.axis_index("section")
    section_count = lax.axis_size("section")
    row_count, shard_width = inputs.shape
    slot_count = weight_tiles.shape[1]
    column_count = shard_width // weight_tiles.shape[2]
    source = source_block[0]
    live_mask = jnp.arange(slot_count, dtype=jnp.int32) < live_slots[0, 0]
    selector = (
        (target_block[0][:, None] == jnp.arange(column_count, dtype=jnp.int32)[None, :])
        & live_mask[:, None]
    ).astype(jnp.float32)

    def compute(gathered):
        return layer_apply(gathered, weight_tiles, source, selector)

    def empty(gathered):
        return jnp.zeros((row_count, shard_width), jnp.bfloat16)

    def step(step_num, current, collected, route):
        gathered = lax.all_gather(current, "neuron", axis=1, tiled=True)
        active = section_pos == step_num
        result = compute(gathered)
        collected = jnp.where(active, result, collected)
        if route is None:
            return (result, collected)
        return (lax.ppermute(result, "section", route), collected)

    collected = jnp.zeros((row_count, shard_width), jnp.bfloat16)
    current = inputs
    if UNROLL:
        for t in range(section_count - 1):
            current, collected = step(t, current, collected, [(t, t + 1)])
    else:
        route = [(i, i + 1) for i in range(section_count - 1)]
        current, collected = lax.fori_loop(
            0, section_count - 1, lambda t, c: step(t, c[0], c[1], route), (current, collected)
        )
    _, collected = step(section_count - 1, current, collected, None)
    return collected[None]


def solution(mesh):
    in_specs = (
        P(None, "neuron"),
        P("section", "neuron", None, None),
        P("section", "neuron"),
        P("section", "neuron"),
        P("section", "neuron"),
    )
    out_specs = P("section", None, "neuron")
    return jax.shard_map(local, mesh=mesh, in_specs=in_specs, out_specs=out_specs, check_vma=False)
```

profile of v0, /device:TPU:455, one launch (start us, length us, event | category | flops | bytes accessed | tf_op | source)
XLA Modules:
  0.0 809.9 jit_solution(16794483580277421957)
XLA Ops:
  0.7 19.8 %all_gather.96 = bf16[6,32768]{1,0:T(8,128)(2,1)S(1)} all-gather(bf16[6,2048]{1,0:T(8,128)(2,1)} %param.5), channel_id=1, replica_groups=mesh['section'=32,'neuron'=16] {'neuron'}, dimensions={1}, use_global_device_ids=true | all-gather | bytes 417792 | tf_op jit(solution)/shard_map/all_gather | solution.py:46
  47.7 16.8 %all_gather.98 = bf16[6,32768]{1,0:T(8,128)(2,1)S(1)} all-gather(bf16[6,2048]{1,0:T(8,128)(2,1)S(1)} %collective-permute-done.1), channel_id=1, replica_groups=mesh['section'=32,'neuron'=16] {'neuron'}, dimensions={1}, use_global_device_ids=true | all-gather | bytes 417792 | tf_op jit(solution)/shard_map/all_gather | solution.py:46
  91.2 16.8 %all_gather.100 = bf16[6,32768]{1,0:T(8,128)(2,1)S(1)} all-gather(bf16[6,2048]{1,0:T(8,128)(2,1)S(1)} %collective-permute-done.3), channel_id=1, replica_groups=mesh['section'=32,'neuron'=16] {'neuron'}, dimensions={1}, use_global_device_ids=true | all-gather | bytes 417792 | tf_op jit(solution)/shard_map/all_gather | solution.py:46
  134.7 16.8 %all_gather.102 = bf16[6,32768]{1,0:T(8,128)(2,1)S(1)} all-gather(bf16[6,2048]{1,0:T(8,128)(2,1)S(1)} %collective-permute-done.5), channel_id=1, replica_groups=mesh['section'=32,'neuron'=16] {'neuron'}, dimensions={1}, use_global_device_ids=true | all-gather | bytes 417792 | tf_op jit(solution)/shard_map/all_gather | solution.py:46
  178.2 17.2 %all_gather.104 = bf16[6,32768]{1,0:T(8,128)(2,1)S(1)} all-gather(bf16[6,2048]{1,0:T(8,128)(2,1)S(1)} %collective-permute-done.7), channel_id=1, replica_groups=mesh['section'=32,'neuron'=16] {'neuron'}, dimensions={1}, use_global_device_ids=true | all-gather | bytes 417792 | tf_op jit(solution)/shard_map/all_gather | solution.py:46
  222.2 16.8 %all_gather.106 = bf16[6,32768]{1,0:T(8,128)(2,1)S(1)} all-gather(bf16[6,2048]{1,0:T(8,128)(2,1)S(1)} %collective-permute-done.9), channel_id=1, replica_groups=mesh['section'=32,'neuron'=16] {'neuron'}, dimensions={1}, use_global_device_ids=true | all-gather | bytes 417792 | tf_op jit(solution)/shard_map/all_gather | solution.py:46
  265.7 16.8 %all_gather.108 = bf16[6,32768]{1,0:T(8,128)(2,1)S(1)} all-gather(bf16[6,2048]{1,0:T(8,128)(2,1)S(1)} %collective-permute-done.11), channel_id=1, replica_groups=mesh['section'=32,'neuron'=16] {'neuron'}, dimensions={1}, use_global_device_ids=true | all-gather | bytes 417792 | tf_op jit(solution)/shard_map/all_gather | solution.py:46
  309.2 16.7 %all_gather.110 = bf16[6,32768]{1,0:T(8,128)(2,1)S(1)} all-gather(bf16[6,2048]{1,0:T(8,128)(2,1)S(1)} %collective-permute-done.13), channel_id=1, replica_groups=mesh['section'=32,'neuron'=16] {'neuron'}, dimensions={1}, use_global_device_ids=true | all-gather | bytes 417792 | tf_op jit(solution)/shard_map/all_gather | solution.py:46
  352.6 16.9 %all_gather.112 = bf16[6,32768]{1,0:T(8,128)(2,1)S(1)} all-gather(bf16[6,2048]{1,0:T(8,128)(2,1)S(1)} %collective-permute-done.15), channel_id=1, replica_groups=mesh['section'=32,'neuron'=16] {'neuron'}, dimensions={1}, use_global_device_ids=true | all-gather | bytes 417792 | tf_op jit(solution)/shard_map/all_gather | solution.py:46
  396.1 16.7 %all_gather.114 = bf16[6,32768]{1,0:T(8,128)(2,1)S(1)} all-gather(bf16[6,2048]{1,0:T(8,128)(2,1)S(1)} %collective-permute-done.17), channel_id=1, replica_groups=mesh['section'=32,'neuron'=16] {'neuron'}, dimensions={1}, use_global_device_ids=true | all-gather | bytes 417792 | tf_op jit(solution)/shard_map/all_gather | solution.py:46
  417.9 16.4 %all_gather.115 = bf16[6,32768]{1,0:T(8,128)(2,1)S(1)} all-gather(bf16[6,2048]{1,0:T(8,128)(2,1)S(1)} %collective-permute-done.18), channel_id=1, replica_groups=mesh['section'=32,'neuron'=16] {'neuron'}, dimensions={1}, use_global_device_ids=true | all-gather | bytes 417792 | tf_op jit(solution)/shard_map/all_gather | solution.py:46
  439.3 16.7 %all_gather.116 = bf16[6,32768]{1,0:T(8,128)(2,1)S(1)} all-gather(bf16[6,2048]{1,0:T(8,128)(2,1)S(1)} %collective-permute-done.19), channel_id=1, replica_groups=mesh['section'=32,'neuron'=16] {'neuron'}, dimensions={1}, use_global_device_ids=true | all-gather | bytes 417792 | tf_op jit(solution)/shard_map/all_gather | solution.py:46
  461.1 16.4 %all_gather.117 = bf16[6,32768]{1,0:T(8,128)(2,1)S(1)} all-gather(bf16[6,2048]{1,0:T(8,128)(2,1)S(1)} %collective-permute-done.20), channel_id=1, replica_groups=mesh['section'=32,'neuron'=16] {'neuron'}, dimensions={1}, use_global_device_ids=true | all-gather | bytes 417792 | tf_op jit(solution)/shard_map/all_gather | solution.py:46
  482.6 16.7 %all_gather.118 = bf16[6,32768]{1,0:T(8,128)(2,1)S(1)} all-gather(bf16[6,2048]{1,0:T(8,128)(2,1)S(1)} %collective-permute-done.21), channel_id=1, replica_groups=mesh['section'=32,'neuron'=16] {'neuron'}, dimensions={1}, use_global_device_ids=true | all-gather | bytes 417792 | tf_op jit(solution)/shard_map/all_gather | solution.py:46
  504.4 16.4 %all_gather.119 = bf16[6,32768]{1,0:T(8,128)(2,1)S(1)} all-gather(bf16[6,2048]{1,0:T(8,128)(2,1)S(1)} %collective-permute-done.22), channel_id=1, replica_groups=mesh['section'=32,'neuron'=16] {'neuron'}, dimensions={1}, use_global_device_ids=true | all-gather | bytes 417792 | tf_op jit(solution)/shard_map/all_gather | solution.py:46
  525.9 16.9 %all_gather.120 = bf16[6,32768]{1,0:T(8,128)(2,1)S(1)} all-gather(bf16[6,2048]{1,0:T(8,128)(2,1)S(1)} %collective-permute-done.23), channel_id=1, replica_groups=mesh['section'=32,'neuron'=16] {'neuron'}, dimensions={1}, use_global_device_ids=true | all-gather | bytes 417792 | tf_op jit(solution)/shard_map/all_gather | solution.py:46
  547.8 16.4 %all_gather.121 = bf16[6,32768]{1,0:T(8,128)(2,1)S(1)} all-gather(bf16[6,2048]{1,0:T(8,128)(2,1)S(1)} %collective-permute-done.24), channel_id=1, replica_groups=mesh['section'=32,'neuron'=16] {'neuron'}, dimensions={1}, use_global_device_ids=true | all-gather | bytes 417792 | tf_op jit(solution)/shard_map/all_gather | solution.py:46
  569.3 16.7 %all_gather.122 = bf16[6,32768]{1,0:T(8,128)(2,1)S(1)} all-gather(bf16[6,2048]{1,0:T(8,128)(2,1)S(1)} %collective-permute-done.25), channel_id=1, replica_groups=mesh['section'=32,'neuron'=16] {'neuron'}, dimensions={1}, use_global_device_ids=true | all-gather | bytes 417792 | tf_op jit(solution)/shard_map/all_gather | solution.py:46
  591.1 16.4 %all_gather.123 = bf16[6,32768]{1,0:T(8,128)(2,1)S(1)} all-gather(bf16[6,2048]{1,0:T(8,128)(2,1)S(1)} %collective-permute-done.26), channel_id=1, replica_groups=mesh['section'=32,'neuron'=16] {'neuron'}, dimensions={1}, use_global_device_ids=true | all-gather | bytes 417792 | tf_op jit(solution)/shard_map/all_gather | solution.py:46
  612.6 16.7 %all_gather.124 = bf16[6,32768]{1,0:T(8,128)(2,1)S(1)} all-gather(bf16[6,2048]{1,0:T(8,128)(2,1)S(1)} %collective-permute-done.27), channel_id=1, replica_groups=mesh['section'=32,'neuron'=16] {'neuron'}, dimensions={1}, use_global_device_ids=true | all-gather | bytes 417792 | tf_op jit(solution)/shard_map/all_gather | solution.py:46
  634.3 16.5 %all_gather.125 = bf16[6,32768]{1,0:T(8,128)(2,1)S(1)} all-gather(bf16[6,2048]{1,0:T(8,128)(2,1)S(1)} %collective-permute-done.28), channel_id=1, replica_groups=mesh['section'=32,'neuron'=16] {'neuron'}, dimensions={1}, use_global_device_ids=true | all-gather | bytes 417792 | tf_op jit(solution)/shard_map/all_gather | solution.py:46
  655.9 16.7 %all_gather.126 = bf16[6,32768]{1,0:T(8,128)(2,1)S(1)} all-gather(bf16[6,2048]{1,0:T(8,128)(2,1)S(1)} %collective-permute-done.29), channel_id=1, replica_groups=mesh['section'=32,'neuron'=16] {'neuron'}, dimensions={1}, use_global_device_ids=true | all-gather | bytes 417792 | tf_op jit(solution)/shard_map/all_gather | solution.py:46
  679.2 107.5 %collective-permute-done.30 = bf16[6,2048]{1,0:T(8,128)(2,1)S(1)} collective-permute-done((bf16[6,2048]{1,0:T(8,128)(2,1)S(1)}, bf16[6,2048]{1,0:T(8,128)(2,1)S(1)}, u32[]{:S(2)}, u32[]{:S(2)}) %collective-permute-start.30) | collective-permute-done | bytes 24608 | tf_op jit(solution)/shard_map/ppermute | solution.py:52
  786.7 17.9 %all_gather.127 = bf16[6,32768]{1,0:T(8,128)(2,1)S(1)} all-gather(bf16[6,2048]{1,0:T(8,128)(2,1)S(1)} %collective-permute-done.30), channel_id=1, replica_groups=mesh['section'=32,'neuron'=16] {'neuron'}, dimensions={1}, use_global_device_ids=true | all-gather | bytes 417792 | tf_op jit(solution)/shard_map/all_gather | solution.py:46
  (224 shorter events, 312.4 us)
Async XLA Ops:
  25.5 0.7 collective-permute-start
  47.0 0.7 collective-permute-start.1
  69.0 0.7 collective-permute-start.2
  90.5 0.7 collective-permute-start.3
  112.5 0.7 collective-permute-start.4
  134.1 0.7 collective-permute-start.5
  156.0 0.7 collective-permute-start.6
  177.6 0.7 collective-permute-start.7
  200.0 0.7 collective-permute-start.8
  221.5 0.7 collective-permute-start.9
  243.5 0.7 collective-permute-start.10
  265.0 0.7 collective-permute-start.11
  330.5 0.7 collective-permute-start.14
  395.4 0.7 collective-permute-start.17
  438.7 0.7 collective-permute-start.19
  460.4 0.7 collective-permute-start.20
  481.9 0.7 collective-permute-start.21
  503.7 0.7 collective-permute-start.22
  525.2 0.7 collective-permute-start.23
  547.2 0.7 collective-permute-start.24
  590.4 0.7 collective-permute-start.26
  611.9 0.7 collective-permute-start.27
  655.2 0.7 collective-permute-start.29
  676.9 109.8 %collective-permute-start.30 = (bf16[6,2048]{1,0:T(8,128)(2,1)S(1)}, bf16[6,2048]{1,0:T(8,128)(2,1)S(1)}, u32[]{:S(2)}, u32[]{:S(2)}) collective-permute-start(bf16[6,2048]{1,0:T(8,128)(2,1)S(1)} %bitcast.647), channel_id=1, source_target_pairs={{480,496},{481,497},{482,498},{483,499},{484,500},{485,501},{486,5... | collective-permute-start | bytes 73736 | tf_op jit(solution)/shard_map/ppermute | solution.py:52
  (10 other events, 111.1 us)
where the time goes:
time: 820 us; the launch traced here: 810 us
  blocking collectives  536 us (65%)
  matrix products  117 us (14%)
  waiting for transfers between devices  108 us (13%)
  local copies, waits for them, and re-layouts  25.1 us (3%)
  starting transfers between devices  21.2 us (3%)
    all_gather x32, blocking collectives, step(): gathered = lax.all_gather(current, 'neuron', axis=1, tiled=True)  536 us
    dot_general x32, matrix products, layer_apply(): jnp.einsum('msk,skj->msj', picked, weight_tiles[0], preferred_element_typ...  108 us
    ppermute x31, waiting for transfers between devices, step(): return (lax.ppermute(result, 'section', route), collected)  108 us
    gather x32, local copies, waits for them, and re-layouts, layer_apply(): picked = shaped.at[:, source].get(mode='promise_in_bounds')  23.9 us
    ppermute x31, starting transfers between devices, step(): return (lax.ppermute(result, 'section', route), collected)  21.2 us
  transfers between devices with their start and end apart: 31, of which 1 were waited for; matrix products, arithmetic and copies ran while one was open for 0% of the time, Pallas kernels for 0%

commit v1 on v0

--- a/solution.py
+++ b/solution.py
@@ -43,7 +43,8 @@
         return jnp.zeros((row_count, shard_width), jnp.bfloat16)
 
     def step(step_num, current, collected, route):
-        gathered = lax.all_gather(current, "neuron", axis=1, tiled=True)
+        copies = jnp.concatenate([current] * lax.axis_size("neuron"), axis=1)
+        gathered = lax.all_to_all(copies, "neuron", 1, 1, tiled=True)
         active = section_pos == step_num
         result = compute(gathered)
         collected = jnp.where(active, result, collected)

time: 820 us -> 1260 us (1.54)
  local copies, waits for them, and re-layouts: 25.1 us -> 349 us
  blocking collectives: 536 us -> 586 us
  waiting for transfers between devices: 108 us -> 157 us
  starting transfers between devices: 21.2 us -> 36.5 us
    all_to_all x0 -> x29, blocking collectives: none -> 586 us  [step(): gathered = lax.all_to_all(copies, 'neuron', 1, 1, tiled=True)]
    all_gather x32 -> x0, blocking collectives: 536 us -> none  [step(): gathered = lax.all_gather(current, 'neuron', axis=1, tiled=True)]
    unnamed x37 -> x515, local copies, waits for them, and re-layouts: 0.37 us -> 302 us
    all_to_all x0 -> x3, waiting for transfers between devices: none -> 48.8 us  [step(): gathered = lax.all_to_all(copies, 'neuron', 1, 1, tiled=True)]
    concatenate x0 -> x32, local copies, waits for them, and re-layouts: none -> 20.2 us  [step(): copies = jnp.concatenate([current] * lax.axis_size('neuron'), axis=1)]
    all_to_all x0 -> x3, starting transfers between devices: none -> 15.3 us  [step(): gathered = lax.all_to_all(copies, 'neuron', 1, 1, tiled=True)]
  transfers between devices with their start and end apart: 31 -> 34, of which waited for: 1 -> 4; matrix products, arithmetic and copies ran while one was open for 0% -> 0% of each run, Pallas kernels for 0% -> 0%
where the time goes in v1:
time: 1260 us; the launch traced here: 1250 us
  blocking collectives  586 us (47%)
  local copies, waits for them, and re-layouts  349 us (28%)
  waiting for transfers between devices  157 us (12%)
  matrix products  117 us (9%)
  starting transfers between devices  36.5 us (3%)
    all_to_all x29, blocking collectives, step(): gathered = lax.all_to_all(copies, 'neuron', 1, 1, tiled=True)  586 us
    unnamed x515, local copies, waits for them, and re-layouts  302 us
    ppermute x31, waiting for transfers between devices, step(): return (lax.ppermute(result, 'section', route), collected)  109 us
    dot_general x32, matrix products, layer_apply(): jnp.einsum('msk,skj->msj', picked, weight_tiles[0], preferred_element_typ...  108 us
    all_to_all x3, waiting for transfers between devices, step(): gathered = lax.all_to_all(copies, 'neuron', 1, 1, tiled=True)  48.8 us
    gather x32, local copies, waits for them, and re-layouts, layer_apply(): picked = shaped.at[:, source].get(mode='promise_in_bounds')  25.9 us
  transfers between devices with their start and end apart: 34, of which 4 were waited for; matrix products, arithmetic and copies ran while one was open for 0% of the time, Pallas kernels for 0%

profile of v1, /device:TPU:455, one launch (start us, length us, event | category | flops | bytes accessed | tf_op | source)
XLA Modules:
  0.0 1249.8 jit_solution(4483261639326516877)
XLA Ops:
  96.6 20.2 %all_to_all.289 = bf16[6,16,2048]{2,0,1:T(8,128)(2,1)S(1)} all-to-all(bf16[6,16,2048]{2,0,1:T(8,128)(2,1)} %bitcast.632), channel_id=1, replica_groups=mesh['section'=32,'neuron'=16] {'neuron'}, dimensions={1} | all-to-all | bytes 786432 | tf_op jit(solution)/shard_map/all_to_all | solution.py:47
  131.7 20.2 %all_to_all.290 = bf16[6,16,2048]{2,0,1:T(8,128)(2,1)S(1)} all-to-all(bf16[6,16,2048]{2,0,1:T(8,128)(2,1)} %bitcast.633), channel_id=1, replica_groups=mesh['section'=32,'neuron'=16] {'neuron'}, dimensions={1} | all-to-all | bytes 786432 | tf_op jit(solution)/shard_map/all_to_all | solution.py:47
  166.7 20.2 %all_to_all.291 = bf16[6,16,2048]{2,0,1:T(8,128)(2,1)S(1)} all-to-all(bf16[6,16,2048]{2,0,1:T(8,128)(2,1)} %bitcast.634), channel_id=1, replica_groups=mesh['section'=32,'neuron'=16] {'neuron'}, dimensions={1} | all-to-all | bytes 786432 | tf_op jit(solution)/shard_map/all_to_all | solution.py:47
  201.8 20.2 %all_to_all.292 = bf16[6,16,2048]{2,0,1:T(8,128)(2,1)S(1)} all-to-all(bf16[6,16,2048]{2,0,1:T(8,128)(2,1)} %bitcast.635), channel_id=1, replica_groups=mesh['section'=32,'neuron'=16] {'neuron'}, dimensions={1} | all-to-all | bytes 786432 | tf_op jit(solution)/shard_map/all_to_all | solution.py:47
  236.8 20.2 %all_to_all.293 = bf16[6,16,2048]{2,0,1:T(8,128)(2,1)S(1)} all-to-all(bf16[6,16,2048]{2,0,1:T(8,128)(2,1)} %bitcast.636), channel_id=1, replica_groups=mesh['section'=32,'neuron'=16] {'neuron'}, dimensions={1} | all-to-all | bytes 786432 | tf_op jit(solution)/shard_map/all_to_all | solution.py:47
  271.9 20.3 %all_to_all.294 = bf16[6,16,2048]{2,0,1:T(8,128)(2,1)S(1)} all-to-all(bf16[6,16,2048]{2,0,1:T(8,128)(2,1)} %bitcast.637), channel_id=1, replica_groups=mesh['section'=32,'neuron'=16] {'neuron'}, dimensions={1} | all-to-all | bytes 786432 | tf_op jit(solution)/shard_map/all_to_all | solution.py:47
  307.1 20.2 %all_to_all.295 = bf16[6,16,2048]{2,0,1:T(8,128)(2,1)S(1)} all-to-all(bf16[6,16,2048]{2,0,1:T(8,128)(2,1)} %bitcast.638), channel_id=1, replica_groups=mesh['section'=32,'neuron'=16] {'neuron'}, dimensions={1} | all-to-all | bytes 786432 | tf_op jit(solution)/shard_map/all_to_all | solution.py:47
  342.2 20.2 %all_to_all.296 = bf16[6,16,2048]{2,0,1:T(8,128)(2,1)S(1)} all-to-all(bf16[6,16,2048]{2,0,1:T(8,128)(2,1)} %bitcast.639), channel_id=1, replica_groups=mesh['section'=32,'neuron'=16] {'neuron'}, dimensions={1} | all-to-all | bytes 786432 | tf_op jit(solution)/shard_map/all_to_all | solution.py:47
  377.2 20.2 %all_to_all.297 = bf16[6,16,2048]{2,0,1:T(8,128)(2,1)S(1)} all-to-all(bf16[6,16,2048]{2,0,1:T(8,128)(2,1)} %bitcast.640), channel_id=1, replica_groups=mesh['section'=32,'neuron'=16] {'neuron'}, dimensions={1} | all-to-all | bytes 786432 | tf_op jit(solution)/shard_map/all_to_all | solution.py:47
  412.3 20.2 %all_to_all.298 = bf16[6,16,2048]{2,0,1:T(8,128)(2,1)S(1)} all-to-all(bf16[6,16,2048]{2,0,1:T(8,128)(2,1)} %bitcast.641), channel_id=1, replica_groups=mesh['section'=32,'neuron'=16] {'neuron'}, dimensions={1} | all-to-all | bytes 786432 | tf_op jit(solution)/shard_map/all_to_all | solution.py:47
  447.3 20.2 %all_to_all.299 = bf16[6,16,2048]{2,0,1:T(8,128)(2,1)S(1)} all-to-all(bf16[6,16,2048]{2,0,1:T(8,128)(2,1)} %bitcast.642), channel_id=1, replica_groups=mesh['section'=32,'neuron'=16] {'neuron'}, dimensions={1} | all-to-all | bytes 786432 | tf_op jit(solution)/shard_map/all_to_all | solution.py:47
  482.4 20.2 %all_to_all.300 = bf16[6,16,2048]{2,0,1:T(8,128)(2,1)S(1)} all-to-all(bf16[6,16,2048]{2,0,1:T(8,128)(2,1)} %bitcast.643), channel_id=1, replica_groups=mesh['section'=32,'neuron'=16] {'neuron'}, dimensions={1} | all-to-all | bytes 786432 | tf_op jit(solution)/shard_map/all_to_all | solution.py:47
  517.5 20.2 %all_to_all.301 = bf16[6,16,2048]{2,0,1:T(8,128)(2,1)S(1)} all-to-all(bf16[6,16,2048]{2,0,1:T(8,128)(2,1)} %bitcast.644), channel_id=1, replica_groups=mesh['section'=32,'neuron'=16] {'neuron'}, dimensions={1} | all-to-all | bytes 786432 | tf_op jit(solution)/shard_map/all_to_all | solution.py:47
  587.8 20.2 %all_to_all.302 = bf16[6,16,2048]{2,0,1:T(8,128)(2,1)S(1)} all-to-all(bf16[6,16,2048]{2,0,1:T(8,128)(2,1)} %bitcast.646), channel_id=1, replica_groups=mesh['section'=32,'neuron'=16] {'neuron'}, dimensions={1} | all-to-all | bytes 786432 | tf_op jit(solution)/shard_map/all_to_all | solution.py:47
  622.8 20.2 %all_to_all.303 = bf16[6,16,2048]{2,0,1:T(8,128)(2,1)S(1)} all-to-all(bf16[6,16,2048]{2,0,1:T(8,128)(2,1)} %bitcast.647), channel_id=1, replica_groups=mesh['section'=32,'neuron'=16] {'neuron'}, dimensions={1} | all-to-all | bytes 786432 | tf_op jit(solution)/shard_map/all_to_all | solution.py:47
  657.9 20.2 %all_to_all.304 = bf16[6,16,2048]{2,0,1:T(8,128)(2,1)S(1)} all-to-all(bf16[6,16,2048]{2,0,1:T(8,128)(2,1)} %bitcast.648), channel_id=1, replica_groups=mesh['section'=32,'neuron'=16] {'neuron'}, dimensions={1} | all-to-all | bytes 786432 | tf_op jit(solution)/shard_map/all_to_all | solution.py:47
  693.0 20.2 %all_to_all.305 = bf16[6,16,2048]{2,0,1:T(8,128)(2,1)S(1)} all-to-all(bf16[6,16,2048]{2,0,1:T(8,128)(2,1)} %bitcast.649), channel_id=1, replica_groups=mesh['section'=32,'neuron'=16] {'neuron'}, dimensions={1} | all-to-all | bytes 786432 | tf_op jit(solution)/shard_map/all_to_all | solution.py:47
  728.0 20.2 %all_to_all.306 = bf16[6,16,2048]{2,0,1:T(8,128)(2,1)S(1)} all-to-all(bf16[6,16,2048]{2,0,1:T(8,128)(2,1)} %bitcast.650), channel_id=1, replica_groups=mesh['section'=32,'neuron'=16] {'neuron'}, dimensions={1} | all-to-all | bytes 786432 | tf_op jit(solution)/shard_map/all_to_all | solution.py:47
  763.1 20.2 %all_to_all.307 = bf16[6,16,2048]{2,0,1:T(8,128)(2,1)S(1)} all-to-all(bf16[6,16,2048]{2,0,1:T(8,128)(2,1)} %bitcast.651), channel_id=1, replica_groups=mesh['section'=32,'neuron'=16] {'neuron'}, dimensions={1} | all-to-all | bytes 786432 | tf_op jit(solution)/shard_map/all_to_all | solution.py:47
  798.1 20.6 %all_to_all.308 = bf16[6,16,2048]{2,0,1:T(8,128)(2,1)S(1)} all-to-all(bf16[6,16,2048]{2,0,1:T(8,128)(2,1)} %bitcast.652), channel_id=1, replica_groups=mesh['section'=32,'neuron'=16] {'neuron'}, dimensions={1} | all-to-all | bytes 786432 | tf_op jit(solution)/shard_map/all_to_all | solution.py:47
  833.6 20.2 %all_to_all.309 = bf16[6,16,2048]{2,0,1:T(8,128)(2,1)S(1)} all-to-all(bf16[6,16,2048]{2,0,1:T(8,128)(2,1)} %bitcast.653), channel_id=1, replica_groups=mesh['section'=32,'neuron'=16] {'neuron'}, dimensions={1} | all-to-all | bytes 786432 | tf_op jit(solution)/shard_map/all_to_all | solution.py:47
  903.7 20.2 %all_to_all.311 = bf16[6,16,2048]{2,0,1:T(8,128)(2,1)S(1)} all-to-all(bf16[6,16,2048]{2,0,1:T(8,128)(2,1)} %bitcast.655), channel_id=1, replica_groups=mesh['section'=32,'neuron'=16] {'neuron'}, dimensions={1} | all-to-all | bytes 786432 | tf_op jit(solution)/shard_map/all_to_all | solution.py:47
  1079.0 20.4 %all_to_all.316 = bf16[6,16,2048]{2,0,1:T(8,128)(2,1)S(1)} all-to-all(bf16[6,16,2048]{2,0,1:T(8,128)(2,1)} %bitcast.660), channel_id=1, replica_groups=mesh['section'=32,'neuron'=16] {'neuron'}, dimensions={1} | all-to-all | bytes 786432 | tf_op jit(solution)/shard_map/all_to_all | solution.py:47
  1105.1 108.5 %collective-permute-done.30 = bf16[6,2048]{1,0:T(8,128)(2,1)S(1)} collective-permute-done((bf16[6,2048]{1,0:T(8,128)(2,1)S(1)}, bf16[6,2048]{1,0:T(8,128)(2,1)S(1)}, u32[]{:S(2)}, u32[]{:S(2)}) %collective-permute-start.30) | collective-permute-done | bytes 24608 | tf_op jit(solution)/shard_map/ppermute | solution.py:53
  (737 shorter events, 674.3 us)
Async XLA Ops:
  21.8 25.0 %all-to-all-start = ((bf16[6,16,2048]{2,0,1:T(8,128)(2,1)}), bf16[6,16,2048]{2,0,1:T(8,128)(2,1)S(1)}, u32[]{:S(2)}, u32[]{:S(2)}) async-start(bf16[6,16,2048]{2,0,1:T(8,128)(2,1)} %bitcast.3), calls=%async_computation | async-start | bytes 1048576 | tf_op jit(solution)/shard_map/all_to_all | solution.py:47
  51.2 0.7 collective-permute-start
  86.2 0.7 collective-permute-start.1
  121.3 0.7 collective-permute-start.2
  156.3 0.7 collective-permute-start.3
  191.4 0.7 collective-permute-start.4
  226.5 0.7 collective-permute-start.5
  261.5 0.7 collective-permute-start.6
  296.7 0.7 collective-permute-start.7
  331.8 0.7 collective-permute-start.8
  366.8 0.7 collective-permute-start.9
  401.9 0.7 collective-permute-start.10
  437.0 0.7 collective-permute-start.11
  472.0 0.7 collective-permute-start.12
  507.1 0.7 collective-permute-start.13
  542.1 0.7 collective-permute-start.14
  552.5 20.4 %all-to-all-start.15 = ((bf16[6,16,2048]{2,0,1:T(8,128)(2,1)}), bf16[6,16,2048]{2,0,1:T(8,128)(2,1)S(1)}, u32[]{:S(2)}, u32[]{:S(2)}) async-start(bf16[6,16,2048]{2,0,1:T(8,128)(2,1)} %bitcast.645), calls=%async_computation.15 | async-start | bytes 1048576 | tf_op jit(solution)/shard_map/all_to_all | solution.py:47
  577.4 0.7 collective-permute-start.15
  612.5 0.7 collective-permute-start.16
  647.5 0.7 collective-permute-start.17
  787.8 0.7 collective-permute-start.21
  893.3 0.7 collective-permute-start.24
  1103.8 109.8 %collective-permute-start.30 = (bf16[6,2048]{1,0:T(8,128)(2,1)S(1)}, bf16[6,2048]{1,0:T(8,128)(2,1)S(1)}, u32[]{:S(2)}, u32[]{:S(2)}) collective-permute-start(bf16[6,2048]{1,0:T(8,128)(2,1)S(1)} %bitcast.770), channel_id=1, source_target_pairs={{480,496},{481,497},{482,498},{483,499},{484,500},{485,501},{486,5... | collective-permute-start | bytes 73736 | tf_op jit(solution)/shard_map/ppermute | solution.py:53
  1223.3 21.1 %all-to-all-start.31 = ((bf16[6,16,2048]{2,0,1:T(8,128)(2,1)}), bf16[6,16,2048]{2,0,1:T(8,128)(2,1)S(1)}, u32[]{:S(2)}, u32[]{:S(2)}) async-start(bf16[6,16,2048]{2,0,1:T(8,128)(2,1)} %bitcast.661), calls=%async_computation.31 | async-start | bytes 1048576 | tf_op jit(solution)/shard_map/all_to_all | solution.py:47
  (12 other events, 108.4 us)
